TPU v7x, 512 devices: a whole 4x8x8 slice. The times are simulated.
512 devices in a mesh: ctx: 128 (over z_hi, x, y), head: 4 (over z_lo, core).
Axes of the slice: x: 4, y: 8, z: 8 (z_hi: 4, z_lo: 2; z = z_hi * 2 + z_lo), core: 2. Of those that a mesh axis runs over, the one named last changes fastest.
Arguments:
- queries: bfloat16 [32768, 4096], P(('ctx', 'head')), may hold values from -200 to 200
- normed_key_state: bfloat16 [32768, 2048], P(('ctx', 'head')), may hold values from -5 to 5
- value_state_rows: bfloat16 [32768, 2048], P(('ctx', 'head')), may hold values from -6 to 6
- output_gradient: bfloat16 [32768, 4096], P(('ctx', 'head')), may hold values from -6 to 6
- doc_start: int32 [32768], P('ctx'), may hold values from 0 to 32767, as said below
Outputs:
- grad_queries: bfloat16 [32768, 4096], P(('ctx', 'head'))
- key_gradient: bfloat16 [32768, 2048], P(('ctx', 'head'))
- value_gradient: bfloat16 [32768, 2048], P(('ctx', 'head'))
Inputs may be any that keep to these rules, and one draw needn't show every extreme that they name: doc_start[t] is the first position of the document that holds token t: doc_start[0] = 0, each doc_start[t] equals t or doc_start[t - 1], and the last token, position 32767, begins a document of its own.
All inputs are finite; a program needn't handle non-finite values.
Results may differ from a plain program's by a relative error of at most 0.007.
Values may be sent and summed in bfloat16 or wider, within the bound.
No kernel may reach another device: no remote copies, remote signals or barrier semaphores. Data moves between devices by JAX's collectives and lax.ppermute only.
A program may use at most 64 MiB of HBM per device.

v0:
```python
import jax
import jax.numpy as jnp
from jax import lax
from jax.sharding import PartitionSpec as P

QUERY_HEADS = 32
KEY_VALUE_HEADS = 16
HEAD_SIZE = 128
WINDOW = 512
SPAN = 2
score_scale = 168.0 ** (-0.5)


def passed_along(block, axis, distance):
    devices = range(lax.axis_size(axis))
    route = [(i - distance, i) for i in devices if i - distance in devices]
    return lax.ppermute(block, axis, route)


def pair_scores(query_heads, key_block):
    return score_scale * jnp.einsum(
        "tgjd,kgd->gjtk", query_heads, key_block, preferred_element_type=jnp.float32
    )


def local(queries, normed_key_state, value_state_rows, output_gradient, doc_start):
    query_loc, key_loc, value_loc, grad_loc = (
        lax.all_to_all(queries, "head", split_axis=1, concat_axis=0, tiled=True),
        lax.all_to_all(normed_key_state, "head", split_axis=1, concat_axis=0, tiled=True),
        lax.all_to_all(value_state_rows, "head", split_axis=1, concat_axis=0, tiled=True),
        lax.all_to_all(output_gradient, "head", split_axis=1, concat_axis=0, tiled=True),
    )
    tok_rows = query_loc.shape[0]
    kv_groups = key_loc.shape[1] // HEAD_SIZE
    group_share = QUERY_HEADS // KEY_VALUE_HEADS
    query_heads = query_loc.reshape(tok_rows, kv_groups, group_share, HEAD_SIZE)
    grad_heads = grad_loc.reshape(tok_rows, kv_groups, group_share, HEAD_SIZE)
    kv_local = jnp.stack([key_loc, value_loc])
    kv_blocks = [kv_local]
    for distance in range(1, SPAN + 1):
        kv_blocks.append(passed_along(kv_local, "ctx", distance))
    shard_index = lax.axis_index("ctx")
    local_iota = jnp.arange(tok_rows, dtype=jnp.int32)
    query_pos = shard_index * tok_rows + local_iota

    def visible(distance):
        key_pos = (shard_index - distance) * tok_rows + local_iota
        return (
            (key_pos[None, :] >= doc_start[:, None])
            & (key_pos[None, :] <= query_pos[:, None])
            & (query_pos[:, None] - key_pos[None, :] < WINDOW)
        )

    def unpack(kv_block):
        return (
            kv_block[0].reshape(tok_rows, kv_groups, HEAD_SIZE),
            kv_block[1].reshape(tok_rows, kv_groups, HEAD_SIZE),
        )

    masks = [visible(distance) for distance in range(SPAN + 1)]
    stat_shape = (kv_groups, group_share, tok_rows)
    running = (
        jnp.full(stat_shape, -jnp.inf, jnp.float32),
        jnp.zeros(stat_shape, jnp.float32),
        jnp.zeros(stat_shape, jnp.float32),
    )
    for distance in range(SPAN + 1):
        gather_key_block, gather_value_block = unpack(kv_blocks[distance])
        gather_masked = jnp.where(
            masks[distance], pair_scores(query_heads, gather_key_block), -jnp.inf
        )
        gather_dprob = jnp.einsum(
            "tgjd,kgd->gjtk", grad_heads, gather_value_block, preferred_element_type=jnp.float32
        )
        new_max = jnp.maximum(running[0], jnp.max(gather_masked, axis=-1))
        factor = jnp.exp(running[0] - new_max)
        weights = jnp.exp(gather_masked - new_max[..., None])
        running = (
            new_max,
            running[1] * factor + jnp.sum(weights, axis=-1),
            running[2] * factor + jnp.sum(weights * gather_dprob, axis=-1),
        )
    log_total = running[0] + jnp.log(running[1])
    delta = running[2] / running[1]
    zero_parts = (
        jnp.zeros((tok_rows, kv_groups, group_share, HEAD_SIZE), jnp.float32),
        jnp.zeros((2, tok_rows, kv_groups * HEAD_SIZE), jnp.float32),
    )
    query_total = zero_parts[0]
    kv_parts = []
    for distance in range(SPAN + 1):
        key_block, value_block = unpack(kv_blocks[distance])
        masked = jnp.where(masks[distance], pair_scores(query_heads, key_block), -jnp.inf)
        prob = jnp.exp(masked - log_total[..., None])
        dprob = jnp.einsum(
            "tgjd,kgd->gjtk", grad_heads, value_block, preferred_element_type=jnp.float32
        )
        dscore = (prob * (dprob - delta[..., None])).astype(jnp.bfloat16)
        prob_half = prob.astype(jnp.bfloat16)
        query_part = score_scale * jnp.einsum(
            "gjtk,kgd->tgjd", dscore, key_block, preferred_element_type=jnp.float32
        )
        key_part = score_scale * jnp.einsum(
            "gjtk,tgjd->kgd", dscore, query_heads, preferred_element_type=jnp.float32
        )
        value_part = jnp.einsum(
            "gjtk,tgjd->kgd", prob_half, grad_heads, preferred_element_type=jnp.float32
        )
        query_part, kv_part = (
            query_part,
            jnp.stack([key_part, value_part]).reshape(2, tok_rows, kv_groups * HEAD_SIZE),
        )
        query_total = query_total + query_part
        kv_parts.append(kv_part)
    kv_total = kv_parts[0]
    for distance in range(1, SPAN + 1):
        kv_total = kv_total + passed_along(kv_parts[distance], "ctx", -distance)
    grad_query_loc = query_total.reshape(tok_rows, kv_groups * group_share * HEAD_SIZE).astype(
        jnp.bfloat16
    )
    grad_key_loc = kv_total[0].astype(jnp.bfloat16)
    grad_value_loc = kv_total[1].astype(jnp.bfloat16)
    return (
        lax.all_to_all(grad_query_loc, "head", split_axis=0, concat_axis=1, tiled=True),
        lax.all_to_all(grad_key_loc, "head", split_axis=0, concat_axis=1, tiled=True),
        lax.all_to_all(grad_value_loc, "head", split_axis=0, concat_axis=1, tiled=True),
    )


def solution(mesh):
    placed = (
        P(("ctx", "head"), None),
        P(("ctx", "head"), None),
        P(("ctx", "head"), None),
        P(("ctx", "head"), None),
        P("ctx"),
    )
    return jax.shard_map(
        local,
        mesh=mesh,
        in_specs=placed,
        out_specs=(P(("ctx", "head"), None), P(("ctx", "head"), None), P(("ctx", "head"), None)),
        check_vma=False,
    )
```

profile of v0, /device:TPU:54, one launch (start us, length us, event | category | flops | bytes accessed | tf_op | source)
XLA Modules:
  0.0 253.9 jit_solution(12213496482902532726)
XLA Ops:
  2.4 3.6 %all-to-all-start = ((bf16[64,4,512]{2,0,1:T(8,128)(2,1)}), bf16[64,4,512]{2,0,1:T(8,128)(2,1)S(1)}, u32[]{:S(2)}, u32[]{:S(2)}) async-start(bf16[64,4,512]{2,0,1:T(8,128)(2,1)} %bitcast.174), calls=%async_computation | async-start | bytes 524288 | tf_op jit(solution)/shard_map/all_to_all | solution.py:29
  7.7 4.3 %all-to-all-done = bf16[64,4,512]{2,0,1:T(8,128)(2,1)S(1)} async-done(((bf16[64,4,512]{2,0,1:T(8,128)(2,1)}), bf16[64,4,512]{2,0,1:T(8,128)(2,1)S(1)}, u32[]{:S(2)}, u32[]{:S(2)}) %all-to-all-start) | async-done | bytes 262176 | tf_op jit(solution)/shard_map/all_to_all | solution.py:29
  12.1 3.4 %all-to-all-start.2 = ((bf16[64,4,512]{2,0,1:T(8,128)(2,1)}), bf16[64,4,512]{2,0,1:T(8,128)(2,1)S(1)}, u32[]{:S(2)}, u32[]{:S(2)}) async-start(bf16[64,4,512]{2,0,1:T(8,128)(2,1)} %bitcast.173), calls=%async_computation.2 | async-start | bytes 524288 | tf_op jit(solution)/shard_map/all_to_all | solution.py:30
  16.3 5.1 %all-to-all-done.2 = bf16[64,4,512]{2,0,1:T(8,128)(2,1)S(1)} async-done(((bf16[64,4,512]{2,0,1:T(8,128)(2,1)}), bf16[64,4,512]{2,0,1:T(8,128)(2,1)S(1)}, u32[]{:S(2)}, u32[]{:S(2)}) %all-to-all-start.2) | async-done | bytes 262176 | tf_op jit(solution)/shard_map/all_to_all | solution.py:30
  21.4 3.5 %all-to-all-start.1 = ((bf16[64,4,1024]{2,0,1:T(8,128)(2,1)}), bf16[64,4,1024]{2,0,1:T(8,128)(2,1)S(1)}, u32[]{:S(2)}, u32[]{:S(2)}) async-start(bf16[64,4,1024]{2,0,1:T(8,128)(2,1)} %bitcast.172), calls=%async_computation.1 | async-start | bytes 1048576 | tf_op jit(solution)/shard_map/all_to_all | solution.py:28
  25.8 7.9 %all-to-all-done.1 = bf16[64,4,1024]{2,0,1:T(8,128)(2,1)S(1)} async-done(((bf16[64,4,1024]{2,0,1:T(8,128)(2,1)}), bf16[64,4,1024]{2,0,1:T(8,128)(2,1)S(1)}, u32[]{:S(2)}, u32[]{:S(2)}) %all-to-all-start.1) | async-done | bytes 524320 | tf_op jit(solution)/shard_map/all_to_all | solution.py:28
  33.7 3.5 %all-to-all-start.3 = ((bf16[64,4,1024]{2,0,1:T(8,128)(2,1)}), bf16[64,4,1024]{2,0,1:T(8,128)(2,1)S(1)}, u32[]{:S(2)}, u32[]{:S(2)}) async-start(bf16[64,4,1024]{2,0,1:T(8,128)(2,1)} %bitcast.171), calls=%async_computation.3 | async-start | bytes 1048576 | tf_op jit(solution)/shard_map/all_to_all | solution.py:31
  38.9 5.3 %collective-permute-start.1 = (bf16[2,256,512]{2,1,0:T(8,128)(2,1)}, bf16[2,256,512]{2,1,0:T(8,128)(2,1)}, u32[]{:S(2)}, u32[]{:S(2)}) collective-permute-start(bf16[2,256,512]{2,1,0:T(8,128)(2,1)} %pad_maximum_fusion.2), channel_id=1, source_target_pairs={{0,8},{4,12},{8,16},{12,20},{16,24},{20,28},{24,32},{28,36},{32,40... | collective-permute-start | bytes 1572872 | tf_op jit(solution)/shard_map/ppermute | solution.py:17
  44.3 3.5 %collective-permute-start = (bf16[2,256,512]{2,1,0:T(8,128)(2,1)}, bf16[2,256,512]{2,1,0:T(8,128)(2,1)}, u32[]{:S(2)}, u32[]{:S(2)}) collective-permute-start(bf16[2,256,512]{2,1,0:T(8,128)(2,1)} %pad_maximum_fusion.2), channel_id=1, source_target_pairs={{0,4},{4,8},{8,12},{12,16},{16,20},{20,24},{24,28},{28,32},{32,36}... | collective-permute-start | bytes 1572872 | tf_op jit(solution)/shard_map/ppermute | solution.py:17
  51.8 2.4 fusion.6
  54.2 14.3 %collective-permute-done.1 = bf16[2,256,512]{2,1,0:T(8,128)(2,1)} collective-permute-done((bf16[2,256,512]{2,1,0:T(8,128)(2,1)}, bf16[2,256,512]{2,1,0:T(8,128)(2,1)}, u32[]{:S(2)}, u32[]{:S(2)}) %collective-permute-start.1) | collective-permute-done | bytes 524320 | tf_op jit(solution)/shard_map/ppermute | solution.py:17
  74.0 5.3 %collective-permute-done = bf16[2,256,512]{2,1,0:T(8,128)(2,1)} collective-permute-done((bf16[2,256,512]{2,1,0:T(8,128)(2,1)}, bf16[2,256,512]{2,1,0:T(8,128)(2,1)}, u32[]{:S(2)}, u32[]{:S(2)}) %collective-permute-start) | collective-permute-done | bytes 524320 | tf_op jit(solution)/shard_map/ppermute | solution.py:17
  98.5 2.1 copy.155
  100.6 6.8 %fusion.2 = (bf16[4,2,256,256]{2,3,1,0:T(8,128)(2,1)S(1)}, bf16[4,2,256,256]{2,3,1,0:T(8,128)(2,1)}, bf16[4,2,256,256]{2,3,1,0:T(8,128)(2,1)}) fusion(f32[4,256,256,2]{2,1,3,0:T(8,128)} %get-tuple-element.31, f32[4,2,256,256]{2,3,1,0:T(8,128)} %copy-done.1, f32[4,2,256]{2,1,0:T(2,128)S(1)} %add_divide_fusion, f32[4,2,256]{2,1,0:T(2,128)S(1)} %get-tuple-element.9, ...), kind=kLoop, calls=%fused_computation.4 | loop fusion | flops 6291456 | bytes 15745024 | tf_op jit(solution)/shard_map/convert_element_type | solution.py:98
  111.3 2.2 pad_maximum_fusion
  113.5 2.3 collective-permute-start.2
  115.8 2.2 pad_maximum_fusion.1
  118.1 5.2 %collective-permute-start.3 = (f32[2,256,512]{2,1,0:T(8,128)}, f32[2,256,512]{2,1,0:T(8,128)}, u32[]{:S(2)}, u32[]{:S(2)}) collective-permute-start(f32[2,256,512]{2,1,0:T(8,128)} %pad_maximum_fusion.1), channel_id=1, source_target_pairs={{8,0},{12,4},{16,8},{20,12},{24,16},{28,20},{32,24},{36,28},{40,32... | collective-permute-start | bytes 3145736 | tf_op jit(solution)/shard_map/ppermute | solution.py:17
  127.4 3.6 %all-to-all-start.4 = ((bf16[4,64,1024]{2,1,0:T(8,128)(2,1)}), bf16[4,64,1024]{2,1,0:T(8,128)(2,1)S(1)}, u32[]{:S(2)}, u32[]{:S(2)}) async-start(bf16[4,64,1024]{2,1,0:T(8,128)(2,1)} %convert_element_type.39), calls=%async_computation.4 | async-start | bytes 1048576 | tf_op jit(solution)/shard_map/all_to_all | solution.py:124
  131.7 42.0 %collective-permute-done.2 = f32[2,256,512]{2,1,0:T(8,128)} collective-permute-done((f32[2,256,512]{2,1,0:T(8,128)}, f32[2,256,512]{2,1,0:T(8,128)}, u32[]{:S(2)}, u32[]{:S(2)}) %collective-permute-start.2) | collective-permute-done | bytes 1048608 | tf_op jit(solution)/shard_map/ppermute | solution.py:17
  173.7 57.3 %collective-permute-done.3 = f32[2,256,512]{2,1,0:T(8,128)} collective-permute-done((f32[2,256,512]{2,1,0:T(8,128)}, f32[2,256,512]{2,1,0:T(8,128)}, u32[]{:S(2)}, u32[]{:S(2)}) %collective-permute-start.3) | collective-permute-done | bytes 1048608 | tf_op jit(solution)/shard_map/ppermute | solution.py:17
  233.5 10.2 %all_to_all.112 = bf16[4,64,512]{2,1,0:T(8,128)(2,1)S(1)} all-to-all(bf16[4,64,512]{2,1,0:T(8,128)(2,1)S(1)} %bitcast.204), channel_id=1, replica_groups=mesh['ctx'=128,'head'=4] {'head'}, dimensions={0} | all-to-all | bytes 524288 | tf_op jit(solution)/shard_map/all_to_all | solution.py:125
  243.8 3.4 %all-to-all-start.6 = ((bf16[4,64,512]{2,1,0:T(8,128)(2,1)}), bf16[4,64,512]{2,1,0:T(8,128)(2,1)S(1)}, u32[]{:S(2)}, u32[]{:S(2)}) async-start(bf16[4,64,512]{2,1,0:T(8,128)(2,1)} %bitcast.57), calls=%async_computation.6 | async-start | bytes 524288 | tf_op jit(solution)/shard_map/all_to_all | solution.py:126
  248.8 4.4 %all-to-all-done.6 = bf16[4,64,512]{2,1,0:T(8,128)(2,1)S(1)} async-done(((bf16[4,64,512]{2,1,0:T(8,128)(2,1)}), bf16[4,64,512]{2,1,0:T(8,128)(2,1)S(1)}, u32[]{:S(2)}, u32[]{:S(2)}) %all-to-all-start.6) | async-done | bytes 262176 | tf_op jit(solution)/shard_map/all_to_all | solution.py:126
  (85 shorter events, 48.9 us)
Async XLA Ops:
  0.6 14.8 %copy-start.13 = (bf16[64,4096]{1,0:T(8,128)(2,1)S(1)}, bf16[64,4096]{1,0:T(8,128)(2,1)}, u32[]{:S(2)}) copy-start(bf16[64,4096]{1,0:T(8,128)(2,1)} %param.5) | copy-start | bytes 1572868
  0.6 24.3 %copy-start.14 = (bf16[64,4096]{1,0:T(8,128)(2,1)S(1)}, bf16[64,4096]{1,0:T(8,128)(2,1)}, u32[]{:S(2)}) copy-start(bf16[64,4096]{1,0:T(8,128)(2,1)} %param.8) | copy-start | bytes 1572868
  2.4 9.6 %all-to-all-start = ((bf16[64,4,512]{2,0,1:T(8,128)(2,1)}), bf16[64,4,512]{2,0,1:T(8,128)(2,1)S(1)}, u32[]{:S(2)}, u32[]{:S(2)}) async-start(bf16[64,4,512]{2,0,1:T(8,128)(2,1)} %bitcast.174), calls=%async_computation | async-start | bytes 524288 | tf_op jit(solution)/shard_map/all_to_all | solution.py:29
  12.1 9.4 %all-to-all-start.2 = ((bf16[64,4,512]{2,0,1:T(8,128)(2,1)}), bf16[64,4,512]{2,0,1:T(8,128)(2,1)S(1)}, u32[]{:S(2)}, u32[]{:S(2)}) async-start(bf16[64,4,512]{2,0,1:T(8,128)(2,1)} %bitcast.173), calls=%async_computation.2 | async-start | bytes 524288 | tf_op jit(solution)/shard_map/all_to_all | solution.py:30
  15.5 21.7 %copy-start.16 = (s32[256]{0:T(256)S(1)}, s32[256]{0:T(256)}, u32[]{:S(2)}) copy-start(s32[256]{0:T(256)} %param.9) | copy-start | bytes 3076
  21.4 12.3 %all-to-all-start.1 = ((bf16[64,4,1024]{2,0,1:T(8,128)(2,1)}), bf16[64,4,1024]{2,0,1:T(8,128)(2,1)S(1)}, u32[]{:S(2)}, u32[]{:S(2)}) async-start(bf16[64,4,1024]{2,0,1:T(8,128)(2,1)} %bitcast.172), calls=%async_computation.1 | async-start | bytes 1048576 | tf_op jit(solution)/shard_map/all_to_all | solution.py:28
  33.7 15.8 %all-to-all-start.3 = ((bf16[64,4,1024]{2,0,1:T(8,128)(2,1)}), bf16[64,4,1024]{2,0,1:T(8,128)(2,1)S(1)}, u32[]{:S(2)}, u32[]{:S(2)}) async-start(bf16[64,4,1024]{2,0,1:T(8,128)(2,1)} %bitcast.171), calls=%async_computation.3 | async-start | bytes 1048576 | tf_op jit(solution)/shard_map/all_to_all | solution.py:31
  38.9 29.6 %collective-permute-start.1 = (bf16[2,256,512]{2,1,0:T(8,128)(2,1)}, bf16[2,256,512]{2,1,0:T(8,128)(2,1)}, u32[]{:S(2)}, u32[]{:S(2)}) collective-permute-start(bf16[2,256,512]{2,1,0:T(8,128)(2,1)} %pad_maximum_fusion.2), channel_id=1, source_target_pairs={{0,8},{4,12},{8,16},{12,20},{16,24},{20,28},{24,32},{28,36},{32,40... | collective-permute-start | bytes 1572872 | tf_op jit(solution)/shard_map/ppermute | solution.py:17
  44.3 35.0 %collective-permute-start = (bf16[2,256,512]{2,1,0:T(8,128)(2,1)}, bf16[2,256,512]{2,1,0:T(8,128)(2,1)}, u32[]{:S(2)}, u32[]{:S(2)}) collective-permute-start(bf16[2,256,512]{2,1,0:T(8,128)(2,1)} %pad_maximum_fusion.2), channel_id=1, source_target_pairs={{0,4},{4,8},{8,12},{12,16},{16,20},{20,24},{24,28},{28,32},{32,36}... | collective-permute-start | bytes 1572872 | tf_op jit(solution)/shard_map/ppermute | solution.py:17
  50.4 1.4 copy-start.12
  84.7 1.5 copy-start.6
  86.2 6.4 %copy-start = (f32[4,2,256,256]{2,3,1,0:T(8,128)}, f32[4,2,256,256]{2,3,1,0:T(8,128)S(1)}, u32[]{:S(2)}) copy-start(f32[4,2,256,256]{2,3,1,0:T(8,128)S(1)} %get-tuple-element.30) | copy-start | bytes 6291460
  86.7 7.1 %copy-start.1 = (f32[4,2,256,256]{2,3,1,0:T(8,128)}, f32[4,2,256,256]{2,3,1,0:T(8,128)S(1)}, u32[]{:S(2)}) copy-start(f32[4,2,256,256]{2,3,1,0:T(8,128)S(1)} %get-tuple-element.26) | copy-start | bytes 6291460
  87.3 1.9 copy-start.11
  89.3 2.0 copy-start.15
  107.4 2.5 copy-start.3
  111.3 11.9 %copy-start.2 = (bf16[4,2,256,256]{2,3,1,0:T(8,128)(2,1)S(1)}, bf16[4,2,256,256]{2,3,1,0:T(8,128)(2,1)}, u32[]{:S(2)}) copy-start(bf16[4,2,256,256]{2,3,1,0:T(8,128)(2,1)} %get-tuple-element.21) | copy-start | bytes 3145732
  113.5 10.3 %copy-start.8 = (bf16[1,256,512]{1,2,0:T(8,128)(2,1)S(1)}, bf16[1,256,512]{1,2,0:T(8,128)(2,1)}, u32[]{:S(2)}) copy-start(bf16[1,256,512]{1,2,0:T(8,128)(2,1)} %copy.127) | copy-start | bytes 786436
  113.5 60.1 %collective-permute-start.2 = (f32[2,256,512]{2,1,0:T(8,128)}, f32[2,256,512]{2,1,0:T(8,128)}, u32[]{:S(2)}, u32[]{:S(2)}) collective-permute-start(f32[2,256,512]{2,1,0:T(8,128)} %pad_maximum_fusion), channel_id=1, source_target_pairs={{4,0},{8,4},{12,8},{16,12},{20,16},{24,20},{28,24},{32,28},{36,32}... | collective-permute-start | bytes 3145736 | tf_op jit(solution)/shard_map/ppermute | solution.py:17
  118.1 112.9 %collective-permute-start.3 = (f32[2,256,512]{2,1,0:T(8,128)}, f32[2,256,512]{2,1,0:T(8,128)}, u32[]{:S(2)}, u32[]{:S(2)}) collective-permute-start(f32[2,256,512]{2,1,0:T(8,128)} %pad_maximum_fusion.1), channel_id=1, source_target_pairs={{8,0},{12,4},{16,8},{20,12},{24,16},{28,20},{32,24},{36,28},{40,32... | collective-permute-start | bytes 3145736 | tf_op jit(solution)/shard_map/ppermute | solution.py:17
  123.9 1.3 copy-start.7
  127.4 103.6 %copy-start.9 = (f32[1,256,512]{2,1,0:T(8,128)S(1)}, f32[1,256,512]{2,1,0:T(8,128)}, u32[]{:S(2)}) copy-start(f32[1,256,512]{2,1,0:T(8,128)} %copy.155) | copy-start | bytes 1572868
  127.4 106.2 %all-to-all-start.4 = ((bf16[4,64,1024]{2,1,0:T(8,128)(2,1)}), bf16[4,64,1024]{2,1,0:T(8,128)(2,1)S(1)}, u32[]{:S(2)}, u32[]{:S(2)}) async-start(bf16[4,64,1024]{2,1,0:T(8,128)(2,1)} %convert_element_type.39), calls=%async_computation.4 | async-start | bytes 1048576 | tf_op jit(solution)/shard_map/all_to_all | solution.py:124
  243.8 9.4 %all-to-all-start.6 = ((bf16[4,64,512]{2,1,0:T(8,128)(2,1)}), bf16[4,64,512]{2,1,0:T(8,128)(2,1)S(1)}, u32[]{:S(2)}, u32[]{:S(2)}) async-start(bf16[4,64,512]{2,1,0:T(8,128)(2,1)} %bitcast.57), calls=%async_computation.6 | async-start | bytes 524288 | tf_op jit(solution)/shard_map/all_to_all | solution.py:126
  (3 other events, 3.4 us)
where the time goes:
time: 255 us; the launch traced here: 254 us
  waiting for transfers between devices  141 us (55%)
  starting transfers between devices  37.3 us (15%)
  local copies, waits for them, and re-layouts  33.3 us (13%)
  matrix products  16.5 us (6%)
  other arithmetic  14.8 us (6%)
  blocking collectives  10.2 us (4%)
    ppermute x4, waiting for transfers between devices, passed_along(): return lax.ppermute(block, axis, route)  119 us
    ppermute x4, starting transfers between devices, passed_along(): return lax.ppermute(block, axis, route)  16.3 us
    all_to_all x1, blocking collectives, local(): lax.all_to_all(grad_key_loc, 'head', split_axis=0, concat_axis=1, tiled=T...  10.2 us
    all_to_all x1, waiting for transfers between devices, local(): lax.all_to_all(queries, 'head', split_axis=1, concat_axis=0, tiled=True)  7.94 us
    another operation x6, local copies, waits for them, and re-layouts, local(): jnp.stack([key_part, value_part])  7.59 us
    slice x4, local copies, waits for them, and re-layouts, unpack(): kv_block[1].reshape(tok_rows, kv_groups, HEAD_SIZE)  7.31 us
    convert_element_type x1, other arithmetic, local(): dscore = (prob * (dprob - delta[..., None])).astype(jnp.bfloat16)  6.79 us
    all_to_all x1, waiting for transfers between devices, local(): lax.all_to_all(value_state_rows, 'head', split_axis=1, concat_axis=0, til...  5.12 us
  transfers between devices with their start and end apart: 10, of which 8 were waited for; matrix products, arithmetic and copies ran while one was open for 11% of the time, Pallas kernels for 0%

commit v1 on v0

--- a/solution.py
+++ b/solution.py
@@ -25,7 +25,12 @@
 
 def local(queries, normed_key_state, value_state_rows, output_gradient, doc_start):
     query_loc, key_loc, value_loc, grad_loc = (
-        lax.all_to_all(queries, "head", split_axis=1, concat_axis=0, tiled=True),
+        jnp.concatenate(
+            lax.all_to_all(
+                jnp.stack(jnp.split(queries, lax.axis_size("head"), axis=1)), "head", 0, 0
+            ),
+            axis=0,
+        ),
         lax.all_to_all(normed_key_state, "head", split_axis=1, concat_axis=0, tiled=True),
         lax.all_to_all(value_state_rows, "head", split_axis=1, concat_axis=0, tiled=True),
         lax.all_to_all(output_gradient, "head", split_axis=1, concat_axis=0, tiled=True),

time: 255 us -> 255 us (level)
    all_to_all x1, waiting for transfers between devices: 7.94 us -> 0.01 us  [local(): lax.all_to_all(jnp.stack(jnp.split(queries, lax.axis_size('head'), axis=1...]
    all_to_all x1, waiting for transfers between devices: 0.01 us -> 7.85 us  [local(): lax.all_to_all(output_gradient, 'head', split_axis=1, concat_axis=0, tile...]
where the time goes in v1:
time: 255 us; the launch traced here: 254 us
  waiting for transfers between devices  141 us (55%)
  starting transfers between devices  37.4 us (15%)
  local copies, waits for them, and re-layouts  32.5 us (13%)
  matrix products  16.5 us (6%)
  other arithmetic  15.7 us (6%)
  blocking collectives  10.3 us (4%)
    ppermute x4, waiting for transfers between devices, passed_along(): return lax.ppermute(block, axis, route)  119 us
    ppermute x4, starting transfers between devices, passed_along(): return lax.ppermute(block, axis, route)  16.3 us
    all_to_all x1, blocking collectives, local(): lax.all_to_all(grad_key_loc, 'head', split_axis=0, concat_axis=1, tiled=T...  10.3 us
    all_to_all x1, waiting for transfers between devices, local(): lax.all_to_all(output_gradient, 'head', split_axis=1, concat_axis=0, tile...  7.85 us
    another operation x6, local copies, waits for them, and re-layouts, local(): jnp.stack([key_part, value_part])  7.57 us
    slice x4, local copies, waits for them, and re-layouts, unpack(): kv_block[1].reshape(tok_rows, kv_groups, HEAD_SIZE)  7.29 us
    convert_element_type x1, other arithmetic, local(): dscore = (prob * (dprob - delta[..., None])).astype(jnp.bfloat16)  6.77 us
    all_to_all x1, waiting for transfers between devices, local(): lax.all_to_all(value_state_rows, 'head', split_axis=1, concat_axis=0, til...  5.13 us
  transfers between devices with their start and end apart: 10, of which 8 were waited for; matrix products, arithmetic and copies ran while one was open for 11% of the time, Pallas kernels for 0%

profile of v1, /device:TPU:54, one launch (start us, length us, event | category | flops | bytes accessed | tf_op | source)
XLA Modules:
  0.0 254.0 jit_solution(2645881485803664817)
XLA Ops:
  2.4 3.6 %all-to-all-start.1 = ((bf16[64,4,512]{2,0,1:T(8,128)(2,1)}), bf16[64,4,512]{2,0,1:T(8,128)(2,1)S(1)}, u32[]{:S(2)}, u32[]{:S(2)}) async-start(bf16[64,4,512]{2,0,1:T(8,128)(2,1)} %bitcast.192), calls=%async_computation.1 | async-start | bytes 524288 | tf_op jit(solution)/shard_map/all_to_all | solution.py:34
  7.7 4.3 %all-to-all-done.1 = bf16[64,4,512]{2,0,1:T(8,128)(2,1)S(1)} async-done(((bf16[64,4,512]{2,0,1:T(8,128)(2,1)}), bf16[64,4,512]{2,0,1:T(8,128)(2,1)S(1)}, u32[]{:S(2)}, u32[]{:S(2)}) %all-to-all-start.1) | async-done | bytes 262176 | tf_op jit(solution)/shard_map/all_to_all | solution.py:34
  12.1 3.4 %all-to-all-start.2 = ((bf16[64,4,512]{2,0,1:T(8,128)(2,1)}), bf16[64,4,512]{2,0,1:T(8,128)(2,1)S(1)}, u32[]{:S(2)}, u32[]{:S(2)}) async-start(bf16[64,4,512]{2,0,1:T(8,128)(2,1)} %bitcast.191), calls=%async_computation.2 | async-start | bytes 524288 | tf_op jit(solution)/shard_map/all_to_all | solution.py:35
  16.3 5.1 %all-to-all-done.2 = bf16[64,4,512]{2,0,1:T(8,128)(2,1)S(1)} async-done(((bf16[64,4,512]{2,0,1:T(8,128)(2,1)}), bf16[64,4,512]{2,0,1:T(8,128)(2,1)S(1)}, u32[]{:S(2)}, u32[]{:S(2)}) %all-to-all-start.2) | async-done | bytes 262176 | tf_op jit(solution)/shard_map/all_to_all | solution.py:35
  21.4 3.6 %all-to-all-start.3 = ((bf16[64,4,1024]{2,0,1:T(8,128)(2,1)}), bf16[64,4,1024]{2,0,1:T(8,128)(2,1)S(1)}, u32[]{:S(2)}, u32[]{:S(2)}) async-start(bf16[64,4,1024]{2,0,1:T(8,128)(2,1)} %bitcast.190), calls=%async_computation.3 | async-start | bytes 1048576 | tf_op jit(solution)/shard_map/all_to_all | solution.py:36
  26.0 7.9 %all-to-all-done.3 = bf16[64,4,1024]{2,0,1:T(8,128)(2,1)S(1)} async-done(((bf16[64,4,1024]{2,0,1:T(8,128)(2,1)}), bf16[64,4,1024]{2,0,1:T(8,128)(2,1)S(1)}, u32[]{:S(2)}, u32[]{:S(2)}) %all-to-all-start.3) | async-done | bytes 524320 | tf_op jit(solution)/shard_map/all_to_all | solution.py:36
  33.8 3.5 %all-to-all-start = ((bf16[4,64,1024]{2,1,0:T(8,128)(2,1)}), bf16[4,64,1024]{2,1,0:T(8,128)(2,1)S(1)}, u32[]{:S(2)}, u32[]{:S(2)}) async-start(bf16[4,64,1024]{2,1,0:T(8,128)(2,1)} %pad_maximum_fusion.2), calls=%async_computation | async-start | bytes 1048576 | tf_op jit(solution)/shard_map/all_to_all | solution.py:29
  39.1 5.3 %collective-permute-start.1 = (bf16[2,256,512]{2,1,0:T(8,128)(2,1)}, bf16[2,256,512]{2,1,0:T(8,128)(2,1)}, u32[]{:S(2)}, u32[]{:S(2)}) collective-permute-start(bf16[2,256,512]{2,1,0:T(8,128)(2,1)} %pad_maximum_fusion.3), channel_id=1, source_target_pairs={{0,8},{4,12},{8,16},{12,20},{16,24},{20,28},{24,32},{28,36},{32,40... | collective-permute-start | bytes 1572872 | tf_op jit(solution)/shard_map/ppermute | solution.py:17
  44.4 3.5 %collective-permute-start = (bf16[2,256,512]{2,1,0:T(8,128)(2,1)}, bf16[2,256,512]{2,1,0:T(8,128)(2,1)}, u32[]{:S(2)}, u32[]{:S(2)}) collective-permute-start(bf16[2,256,512]{2,1,0:T(8,128)(2,1)} %pad_maximum_fusion.3), channel_id=1, source_target_pairs={{0,4},{4,8},{8,12},{12,16},{16,20},{20,24},{24,28},{28,32},{32,36}... | collective-permute-start | bytes 1572872 | tf_op jit(solution)/shard_map/ppermute | solution.py:17
  51.9 2.4 fusion.6
  54.3 14.3 %collective-permute-done.1 = bf16[2,256,512]{2,1,0:T(8,128)(2,1)} collective-permute-done((bf16[2,256,512]{2,1,0:T(8,128)(2,1)}, bf16[2,256,512]{2,1,0:T(8,128)(2,1)}, u32[]{:S(2)}, u32[]{:S(2)}) %collective-permute-start.1) | collective-permute-done | bytes 524320 | tf_op jit(solution)/shard_map/ppermute | solution.py:17
  74.1 5.3 %collective-permute-done = bf16[2,256,512]{2,1,0:T(8,128)(2,1)} collective-permute-done((bf16[2,256,512]{2,1,0:T(8,128)(2,1)}, bf16[2,256,512]{2,1,0:T(8,128)(2,1)}, u32[]{:S(2)}, u32[]{:S(2)}) %collective-permute-start) | collective-permute-done | bytes 524320 | tf_op jit(solution)/shard_map/ppermute | solution.py:17
  97.4 2.1 copy.152
  100.7 6.8 %fusion.2 = (bf16[4,2,256,256]{2,3,1,0:T(8,128)(2,1)S(1)}, bf16[4,2,256,256]{2,3,1,0:T(8,128)(2,1)}, bf16[4,2,256,256]{2,3,1,0:T(8,128)(2,1)}) fusion(f32[4,256,256,2]{2,1,3,0:T(8,128)} %get-tuple-element.35, f32[4,2,256,256]{2,3,1,0:T(8,128)} %copy-done.1, f32[4,2,256]{2,1,0:T(2,128)S(1)} %add_divide_fusion, f32[4,2,256]{2,1,0:T(2,128)S(1)} %get-tuple-element.9, ...), kind=kLoop, calls=%fused_computation.4 | loop fusion | flops 6291456 | bytes 15745024 | tf_op jit(solution)/shard_map/convert_element_type | solution.py:103
  111.5 2.2 pad_maximum_fusion
  113.6 2.3 collective-permute-start.2
  115.9 2.2 pad_maximum_fusion.1
  118.2 5.2 %collective-permute-start.3 = (f32[2,256,512]{2,1,0:T(8,128)}, f32[2,256,512]{2,1,0:T(8,128)}, u32[]{:S(2)}, u32[]{:S(2)}) collective-permute-start(f32[2,256,512]{2,1,0:T(8,128)} %pad_maximum_fusion.1), channel_id=1, source_target_pairs={{8,0},{12,4},{16,8},{20,12},{24,16},{28,20},{32,24},{36,28},{40,32... | collective-permute-start | bytes 3145736 | tf_op jit(solution)/shard_map/ppermute | solution.py:17
  127.5 3.6 %all-to-all-start.4 = ((bf16[4,64,1024]{2,1,0:T(8,128)(2,1)}), bf16[4,64,1024]{2,1,0:T(8,128)(2,1)S(1)}, u32[]{:S(2)}, u32[]{:S(2)}) async-start(bf16[4,64,1024]{2,1,0:T(8,128)(2,1)} %convert_element_type.39), calls=%async_computation.4 | async-start | bytes 1048576 | tf_op jit(solution)/shard_map/all_to_all | solution.py:129
  131.8 42.0 %collective-permute-done.2 = f32[2,256,512]{2,1,0:T(8,128)} collective-permute-done((f32[2,256,512]{2,1,0:T(8,128)}, f32[2,256,512]{2,1,0:T(8,128)}, u32[]{:S(2)}, u32[]{:S(2)}) %collective-permute-start.2) | collective-permute-done | bytes 1048608 | tf_op jit(solution)/shard_map/ppermute | solution.py:17
  173.8 57.2 %collective-permute-done.3 = f32[2,256,512]{2,1,0:T(8,128)} collective-permute-done((f32[2,256,512]{2,1,0:T(8,128)}, f32[2,256,512]{2,1,0:T(8,128)}, u32[]{:S(2)}, u32[]{:S(2)}) %collective-permute-start.3) | collective-permute-done | bytes 1048608 | tf_op jit(solution)/shard_map/ppermute | solution.py:17
  233.6 10.3 %all_to_all.101 = bf16[4,64,512]{2,1,0:T(8,128)(2,1)S(1)} all-to-all(bf16[4,64,512]{2,1,0:T(8,128)(2,1)S(1)} %bitcast.221), channel_id=1, replica_groups=mesh['ctx'=128,'head'=4] {'head'}, dimensions={0} | all-to-all | bytes 524288 | tf_op jit(solution)/shard_map/all_to_all | solution.py:130
  243.9 3.4 %all-to-all-start.6 = ((bf16[4,64,512]{2,1,0:T(8,128)(2,1)}), bf16[4,64,512]{2,1,0:T(8,128)(2,1)S(1)}, u32[]{:S(2)}, u32[]{:S(2)}) async-start(bf16[4,64,512]{2,1,0:T(8,128)(2,1)} %bitcast.60), calls=%async_computation.6 | async-start | bytes 524288 | tf_op jit(solution)/shard_map/all_to_all | solution.py:131
  248.8 4.4 %all-to-all-done.6 = bf16[4,64,512]{2,1,0:T(8,128)(2,1)S(1)} async-done(((bf16[4,64,512]{2,1,0:T(8,128)(2,1)}), bf16[4,64,512]{2,1,0:T(8,128)(2,1)S(1)}, u32[]{:S(2)}, u32[]{:S(2)}) %all-to-all-start.6) | async-done | bytes 262176 | tf_op jit(solution)/shard_map/all_to_all | solution.py:131
  (86 shorter events, 49.0 us)
Async XLA Ops:
  0.6 14.8 %copy-start.13 = (bf16[64,4096]{1,0:T(8,128)(2,1)S(1)}, bf16[64,4096]{1,0:T(8,128)(2,1)}, u32[]{:S(2)}) copy-start(bf16[64,4096]{1,0:T(8,128)(2,1)} %param.8) | copy-start | bytes 1572868
  0.6 24.4 %copy-start.14 = (bf16[64,4096]{1,0:T(8,128)(2,1)S(1)}, bf16[64,4096]{1,0:T(8,128)(2,1)}, u32[]{:S(2)}) copy-start(bf16[64,4096]{1,0:T(8,128)(2,1)} %param.5) | copy-start | bytes 1572868
  2.4 9.6 %all-to-all-start.1 = ((bf16[64,4,512]{2,0,1:T(8,128)(2,1)}), bf16[64,4,512]{2,0,1:T(8,128)(2,1)S(1)}, u32[]{:S(2)}, u32[]{:S(2)}) async-start(bf16[64,4,512]{2,0,1:T(8,128)(2,1)} %bitcast.192), calls=%async_computation.1 | async-start | bytes 524288 | tf_op jit(solution)/shard_map/all_to_all | solution.py:34
  12.1 9.4 %all-to-all-start.2 = ((bf16[64,4,512]{2,0,1:T(8,128)(2,1)}), bf16[64,4,512]{2,0,1:T(8,128)(2,1)S(1)}, u32[]{:S(2)}, u32[]{:S(2)}) async-start(bf16[64,4,512]{2,0,1:T(8,128)(2,1)} %bitcast.191), calls=%async_computation.2 | async-start | bytes 524288 | tf_op jit(solution)/shard_map/all_to_all | solution.py:35
  21.4 15.9 %copy-start.16 = (s32[256]{0:T(256)S(1)}, s32[256]{0:T(256)}, u32[]{:S(2)}) copy-start(s32[256]{0:T(256)} %param.9) | copy-start | bytes 3076
  21.4 12.4 %all-to-all-start.3 = ((bf16[64,4,1024]{2,0,1:T(8,128)(2,1)}), bf16[64,4,1024]{2,0,1:T(8,128)(2,1)S(1)}, u32[]{:S(2)}, u32[]{:S(2)}) async-start(bf16[64,4,1024]{2,0,1:T(8,128)(2,1)} %bitcast.190), calls=%async_computation.3 | async-start | bytes 1048576 | tf_op jit(solution)/shard_map/all_to_all | solution.py:36
  33.8 15.8 %all-to-all-start = ((bf16[4,64,1024]{2,1,0:T(8,128)(2,1)}), bf16[4,64,1024]{2,1,0:T(8,128)(2,1)S(1)}, u32[]{:S(2)}, u32[]{:S(2)}) async-start(bf16[4,64,1024]{2,1,0:T(8,128)(2,1)} %pad_maximum_fusion.2), calls=%async_computation | async-start | bytes 1048576 | tf_op jit(solution)/shard_map/all_to_all | solution.py:29
  39.1 29.6 %collective-permute-start.1 = (bf16[2,256,512]{2,1,0:T(8,128)(2,1)}, bf16[2,256,512]{2,1,0:T(8,128)(2,1)}, u32[]{:S(2)}, u32[]{:S(2)}) collective-permute-start(bf16[2,256,512]{2,1,0:T(8,128)(2,1)} %pad_maximum_fusion.3), channel_id=1, source_target_pairs={{0,8},{4,12},{8,16},{12,20},{16,24},{20,28},{24,32},{28,36},{32,40... | collective-permute-start | bytes 1572872 | tf_op jit(solution)/shard_map/ppermute | solution.py:17
  44.4 35.0 %collective-permute-start = (bf16[2,256,512]{2,1,0:T(8,128)(2,1)}, bf16[2,256,512]{2,1,0:T(8,128)(2,1)}, u32[]{:S(2)}, u32[]{:S(2)}) collective-permute-start(bf16[2,256,512]{2,1,0:T(8,128)(2,1)} %pad_maximum_fusion.3), channel_id=1, source_target_pairs={{0,4},{4,8},{8,12},{12,16},{16,20},{20,24},{24,28},{28,32},{32,36}... | collective-permute-start | bytes 1572872 | tf_op jit(solution)/shard_map/ppermute | solution.py:17
  50.6 1.4 copy-start.12
  84.8 1.5 copy-start.6
  86.3 5.1 %copy-start = (f32[4,2,256,256]{2,3,1,0:T(8,128)}, f32[4,2,256,256]{2,3,1,0:T(8,128)S(1)}, u32[]{:S(2)}) copy-start(f32[4,2,256,256]{2,3,1,0:T(8,128)S(1)} %get-tuple-element.34) | copy-start | bytes 6291460
  86.9 7.2 %copy-start.1 = (f32[4,2,256,256]{2,3,1,0:T(8,128)}, f32[4,2,256,256]{2,3,1,0:T(8,128)S(1)}, u32[]{:S(2)}) copy-start(f32[4,2,256,256]{2,3,1,0:T(8,128)S(1)} %get-tuple-element.30) | copy-start | bytes 6291460
  87.5 1.9 copy-start.11
  89.4 2.0 copy-start.15
  107.5 2.5 copy-start.3
  111.5 11.9 %copy-start.2 = (bf16[4,2,256,256]{2,3,1,0:T(8,128)(2,1)S(1)}, bf16[4,2,256,256]{2,3,1,0:T(8,128)(2,1)}, u32[]{:S(2)}) copy-start(bf16[4,2,256,256]{2,3,1,0:T(8,128)(2,1)} %get-tuple-element.25) | copy-start | bytes 3145732
  113.6 10.3 %copy-start.8 = (bf16[1,256,512]{1,2,0:T(8,128)(2,1)S(1)}, bf16[1,256,512]{1,2,0:T(8,128)(2,1)}, u32[]{:S(2)}) copy-start(bf16[1,256,512]{1,2,0:T(8,128)(2,1)} %copy.124) | copy-start | bytes 786436
  113.6 60.1 %collective-permute-start.2 = (f32[2,256,512]{2,1,0:T(8,128)}, f32[2,256,512]{2,1,0:T(8,128)}, u32[]{:S(2)}, u32[]{:S(2)}) collective-permute-start(f32[2,256,512]{2,1,0:T(8,128)} %pad_maximum_fusion), channel_id=1, source_target_pairs={{4,0},{8,4},{12,8},{16,12},{20,16},{24,20},{28,24},{32,28},{36,32}... | collective-permute-start | bytes 3145736 | tf_op jit(solution)/shard_map/ppermute | solution.py:17
  118.2 112.9 %collective-permute-start.3 = (f32[2,256,512]{2,1,0:T(8,128)}, f32[2,256,512]{2,1,0:T(8,128)}, u32[]{:S(2)}, u32[]{:S(2)}) collective-permute-start(f32[2,256,512]{2,1,0:T(8,128)} %pad_maximum_fusion.1), channel_id=1, source_target_pairs={{8,0},{12,4},{16,8},{20,12},{24,16},{28,20},{32,24},{36,28},{40,32... | collective-permute-start | bytes 3145736 | tf_op jit(solution)/shard_map/ppermute | solution.py:17
  124.0 1.3 copy-start.7
  127.5 103.6 %copy-start.9 = (f32[1,256,512]{2,1,0:T(8,128)S(1)}, f32[1,256,512]{2,1,0:T(8,128)}, u32[]{:S(2)}) copy-start(f32[1,256,512]{2,1,0:T(8,128)} %copy.152) | copy-start | bytes 1572868
  127.5 106.1 %all-to-all-start.4 = ((bf16[4,64,1024]{2,1,0:T(8,128)(2,1)}), bf16[4,64,1024]{2,1,0:T(8,128)(2,1)S(1)}, u32[]{:S(2)}, u32[]{:S(2)}) async-start(bf16[4,64,1024]{2,1,0:T(8,128)(2,1)} %convert_element_type.39), calls=%async_computation.4 | async-start | bytes 1048576 | tf_op jit(solution)/shard_map/all_to_all | solution.py:129
  243.9 9.4 %all-to-all-start.6 = ((bf16[4,64,512]{2,1,0:T(8,128)(2,1)}), bf16[4,64,512]{2,1,0:T(8,128)(2,1)S(1)}, u32[]{:S(2)}, u32[]{:S(2)}) async-start(bf16[4,64,512]{2,1,0:T(8,128)(2,1)} %bitcast.60), calls=%async_computation.6 | async-start | bytes 524288 | tf_op jit(solution)/shard_map/all_to_all | solution.py:131
  (3 other events, 3.4 us)
